TPU v7x, 256 devices: a whole 4x4x8 slice. The times are simulated.
256 devices in a mesh: scen: 64 (over y, x, z_hi, core), trade: 4 (over z_lo).
Axes of the slice: x: 4, y: 4, z: 8 (z_hi: 2, z_lo: 4; z = z_hi * 4 + z_lo), core: 2. Of those that a mesh axis runs over, the one named last changes fastest.
Arguments:
- payoffs: float32 [12, 12, 12, 4, 8192], P(None, None, None, 'trade', 'scen'), may hold values from -4 to 4
- sweep_counts: int32 [4, 8192], P('trade', 'scen'), may hold values from 1 to 6
- netting_map: int32 [4, 8192], P('trade'), may hold values from 0 to 511
- type_lengths: int32 [8], replicated, may hold values from 1 to 8192, 32768 in all
- type_diffusion: float32 [8], replicated, may hold values from 0.02 to 0.15
- type_discount: float32 [8], replicated, may hold values from 0.01 to 0.12
- factors: float32 [3, 8192], P(None, 'scen'), may hold values from -1 to 1
Outputs:
- exposures: float32 [8192, 512], P('scen', 'trade')
- allocation: float32 [4, 8192], P('trade', 'scen')
All inputs are finite; a program needn't handle non-finite values.
Results may differ from a plain program's by a relative error of at most 0.0055.
Values may be sent and summed in bfloat16 or wider, within the bound.
No kernel may reach another device: no remote copies, remote signals or barrier semaphores. Data moves between devices by JAX's collectives and lax.ppermute only.
A program may use at most 128 MiB of HBM per device.

v0:
```python
import jax
import jax.numpy as jnp
from jax import lax
from jax.sharding import Mesh, PartitionSpec as P

GRID = 12
NETS = 512
TYPES = 8
MAX_SWEEPS = 6


def cheb_matrix():
    intervals = GRID - 1
    order_index = jnp.arange(GRID, dtype=jnp.float32)
    end_weights = jnp.where((order_index == 0) | (order_index == intervals), 0.5, 1.0).astype(
        jnp.float32
    )
    angles = jnp.pi * order_index[:, None] * order_index[None, :] / intervals
    return 2.0 / intervals * end_weights[:, None] * end_weights[None, :] * jnp.cos(angles)


def cheb_basis(factors):
    factor_basis = []
    for column in range(3):
        point = factors[column]
        recurrence = [jnp.ones_like(point), point]
        for degree in range(2, GRID):
            recurrence.append(2.0 * point * recurrence[-1] - recurrence[-2])
        factor_basis.append(jnp.stack(recurrence[:GRID], 0))
    product = factor_basis[0][:, None, None, :] * factor_basis[1][None, :, None, :]
    product = product * factor_basis[2][None, None, :, :]
    return product.reshape(GRID * GRID * GRID, -1).astype(jnp.bfloat16)


def price(grid_values, counts, trade_index, type_lengths, type_diffusion, type_discount):
    type_ends = jnp.cumsum(type_lengths)
    type_ids = jnp.sum((trade_index[:, None] >= type_ends[None, :]).astype(jnp.int32), axis=1)
    type_hot = (type_ids[:, None] == jnp.arange(TYPES, dtype=jnp.int32)[None, :]).astype(
        jnp.float32
    )
    diffusion = jnp.sum(type_hot * type_diffusion[None, :], axis=1)
    discount = jnp.sum(type_hot * type_discount[None, :], axis=1)

    def smooth_step(degree, field):
        padded = jnp.pad(field, ((1, 1), (1, 1), (1, 1), (0, 0)))
        beside = padded[2:, 1:-1, 1:-1] + padded[:-2, 1:-1, 1:-1]
        beside = beside + padded[1:-1, 2:, 1:-1] + padded[1:-1, :-2, 1:-1]
        beside = beside + padded[1:-1, 1:-1, 2:] + padded[1:-1, 1:-1, :-2]
        updated = field + diffusion * (beside - 6.0 * field) - discount * field
        return jnp.where(degree < counts, updated, field)

    field = lax.fori_loop(0, MAX_SWEEPS, smooth_step, grid_values)
    matrix = cheb_matrix()
    field = jnp.einsum("ai,ijlp->ajlp", matrix, field, precision=lax.Precision.HIGHEST)
    field = jnp.einsum("bj,ajlp->ablp", matrix, field, precision=lax.Precision.HIGHEST)
    field = jnp.einsum("cl,ablp->abcp", matrix, field, precision=lax.Precision.HIGHEST)
    return field.reshape(GRID * GRID * GRID, -1).astype(jnp.bfloat16)


SCEN_PARTS = (("y", 4), ("x", 4), ("zh", 2), ("core", 2))
SCEN = tuple(name for name, _ in SCEN_PARTS)
SIZES = dict(SCEN_PARTS)
def shifted(value, name, count, shift):
    return lax.ppermute(value, name, [(j, (j + shift) % count) for j in range(count)])


def axis_scatter_sum(part, name):
    count = SIZES[name]
    own = lax.axis_index(name)
    blocks = part.reshape((count, part.shape[0] // count) + part.shape[1:])
    total = lax.dynamic_index_in_dim(blocks, own, 0, keepdims=False)
    for shift in range(1, count):
        sent = lax.dynamic_index_in_dim(blocks, (own + shift) % count, 0, keepdims=False)
        total = total + shifted(sent, name, count, shift)
    return total


def axis_gather(block, name):
    count = SIZES[name]
    own = lax.axis_index(name)
    rows = block.shape[0]
    whole = jnp.zeros((count * rows,) + block.shape[1:], block.dtype)
    whole = lax.dynamic_update_slice_in_dim(whole, block, own * rows, 0)
    for shift in range(1, count):
        got = shifted(block, name, count, shift)
        whole = lax.dynamic_update_slice_in_dim(whole, got, ((own - shift) % count) * rows, 0)
    return whole


def pair_sum(part, name):
    return part + lax.ppermute(part, name, [(0, 1), (1, 0)])


def scen_sum(part):
    part = pair_sum(part, "core")
    part = axis_scatter_sum(part, "x")
    part = axis_scatter_sum(part, "y")
    part = pair_sum(part, "zh")
    part = axis_gather(part, "y")
    return axis_gather(part, "x")


def shards(
    payoffs, sweep_counts, netting_map, type_lengths, type_diffusion, type_discount, factors
):
    trades_here = payoffs.shape[4]
    scen_index = lax.axis_index(SCEN)
    group_index = lax.axis_index("trade")
    block_size = trades_here * lax.axis_size(SCEN)
    first_trade = group_index * block_size + scen_index * trades_here
    trade_index = first_trade + jnp.arange(trades_here, dtype=jnp.int32)
    coef_local = price(
        payoffs[:, :, :, 0, :],
        sweep_counts[0],
        trade_index,
        type_lengths,
        type_diffusion,
        type_discount,
    )
    own_sets = lax.dynamic_slice_in_dim(netting_map[0], scen_index * trades_here, trades_here)
    rows = coef_local.shape[0]
    sent = jnp.concatenate(
        [
            coef_local,
            (own_sets // 32).astype(jnp.bfloat16)[None],
            (own_sets % 32).astype(jnp.bfloat16)[None],
            jnp.zeros((6, trades_here), jnp.bfloat16),
        ],
        axis=0,
    )
    groups = lax.axis_size("trade")
    got = jnp.concatenate(
        [sent] + [shifted(sent, "trade", groups, d) for d in range(1, groups)], axis=1
    )
    coef_rows = got[:rows]
    set_ids = got[rows].astype(jnp.int32) * 32 + got[rows + 1].astype(jnp.int32)
    sets_here = NETS // lax.axis_size("trade")
    classes = group_index * sets_here + jnp.arange(sets_here, dtype=jnp.int32)
    set_hot = (set_ids[:, None] == classes[None, :]).astype(jnp.bfloat16)
    set_part = jnp.dot(coef_rows, set_hot, preferred_element_type=jnp.float32)
    set_coef = scen_sum(set_part)
    basis_rows = cheb_basis(factors).astype(jnp.float32)
    totals = lax.dot_general(
        basis_rows,
        set_coef,
        (((0,), (0,)), ((), ())),
        precision=lax.Precision.HIGHEST,
    )
    exposures = jnp.maximum(totals, 0.0)
    scen_total = factors.shape[1] * lax.axis_size(SCEN)
    weight_part = jnp.dot(basis_rows, exposures, precision=lax.Precision.HIGHEST)
    weights = scen_sum(weight_part) / scen_total
    trade_weights = lax.dot_general(
        coef_rows.astype(jnp.float32),
        weights,
        (((0,), (0,)), ((), ())),
        precision=lax.Precision.HIGHEST,
    )
    alloc_terms = jnp.sum(trade_weights * set_hot.astype(jnp.float32), axis=1)
    alloc_terms = alloc_terms.reshape(groups, trades_here)
    allocation = alloc_terms[0]
    for d in range(1, groups):
        allocation = allocation + shifted(alloc_terms[d], "trade", groups, -d)
    return (exposures, allocation.reshape(1, trades_here))


def solution(mesh):
    parts = mesh.devices.reshape(tuple(size for _, size in SCEN_PARTS) + (mesh.shape["trade"],))
    fine = Mesh(parts, SCEN + ("trade",))
    return jax.shard_map(
        shards,
        mesh=fine,
        in_specs=(
            P(None, None, None, "trade", SCEN),
            P("trade", SCEN),
            P("trade", None),
            P(),
            P(),
            P(),
            P(None, SCEN),
        ),
        out_specs=(P(SCEN, "trade"), P("trade", SCEN)),
        check_vma=False,
    )
```

profile of v0, /device:TPU:2, one launch (start us, length us, event | category | flops | bytes accessed | tf_op | source)
XLA Modules:
  0.0 177.5 jit_solution(1884074211495557057)
XLA Ops:
  4.3 5.0 %while.15 = (s32[]{:T(128)}, f32[12,12,12,128]{3,2,1,0:T(8,128)S(1)}, s32[128]{0:T(128)S(1)}, f32[128]{0:T(128)S(1)}, f32[128]{0:T(128)S(1)}, /*index=5*/s32[]{:T(128)}) while((s32[]{:T(128)}, f32[12,12,12,128]{3,2,1,0:T(8,128)S(1)}, s32[128]{0:T(128)S(1)}, f32[128]{0:T(128)S(1)}, f32[128]{0:T(128)S(1)}, /*index=5*/s32[]{:T(128)}) %tuple.94), condition=%wide.region_5.6_spmd, body=%wide.region_4.5_spmd.sunk | while | flops 2654338 | bytes 3540809 | solution.py:52
  16.5 3.3 %collective-permute-start.1 = (bf16[1736,128]{1,0:T(8,128)(2,1)S(1)}, bf16[1736,128]{1,0:T(8,128)(2,1)S(1)}, u32[]{:S(2)}, u32[]{:S(2)}) collective-permute-start(bf16[1736,128]{1,0:T(8,128)(2,1)S(1)} %concatenate.6), channel_id=1, source_target_pairs={{0,2},{1,3},{2,0},{3,1},{4,6},{5,7},{6,4},{7,5},{8,10},{9,11},{10,... | collective-permute-start | bytes 1333256 | tf_op jit(solution)/shard_map/ppermute | solution.py:64
  20.8 9.6 %collective-permute-done = bf16[1736,128]{1,0:T(8,128)(2,1)S(1)} collective-permute-done((bf16[1736,128]{1,0:T(8,128)(2,1)S(1)}, bf16[1736,128]{1,0:T(8,128)(2,1)S(1)}, u32[]{:S(2)}, u32[]{:S(2)}) %collective-permute-start) | collective-permute-done | bytes 444448 | tf_op jit(solution)/shard_map/ppermute | solution.py:64
  30.4 18.2 %collective-permute-done.1 = bf16[1736,128]{1,0:T(8,128)(2,1)S(1)} collective-permute-done((bf16[1736,128]{1,0:T(8,128)(2,1)S(1)}, bf16[1736,128]{1,0:T(8,128)(2,1)S(1)}, u32[]{:S(2)}, u32[]{:S(2)}) %collective-permute-start.1) | collective-permute-done | bytes 444448 | tf_op jit(solution)/shard_map/ppermute | solution.py:64
  50.1 2.4 %collective-permute-done.3 = f32[1728,128]{1,0:T(8,128)S(1)} collective-permute-done((f32[1728,128]{1,0:T(8,128)S(1)}, f32[1728,128]{1,0:T(8,128)S(1)}, u32[]{:S(2)}, u32[]{:S(2)}) %collective-permute-start.3) | collective-permute-done | bytes 884768 | tf_op jit(solution)/shard_map/ppermute | solution.py:91
  57.6 3.5 %collective-permute-done.4 = f32[432,128]{1,0:T(8,128)S(1)} collective-permute-done((f32[432,128]{1,0:T(8,128)S(1)}, f32[432,128]{1,0:T(8,128)S(1)}, u32[]{:S(2)}, u32[]{:S(2)}) %collective-permute-start.4) | collective-permute-done | bytes 221216 | tf_op jit(solution)/shard_map/ppermute | solution.py:64
  61.1 3.0 %collective-permute-done.5 = f32[432,128]{1,0:T(8,128)S(1)} collective-permute-done((f32[432,128]{1,0:T(8,128)S(1)}, f32[432,128]{1,0:T(8,128)S(1)}, u32[]{:S(2)}, u32[]{:S(2)}) %collective-permute-start.5) | collective-permute-done | bytes 221216 | tf_op jit(solution)/shard_map/ppermute | solution.py:64
  64.1 2.9 %collective-permute-done.6 = f32[432,128]{1,0:T(8,128)S(1)} collective-permute-done((f32[432,128]{1,0:T(8,128)S(1)}, f32[432,128]{1,0:T(8,128)S(1)}, u32[]{:S(2)}, u32[]{:S(2)}) %collective-permute-start.6) | collective-permute-done | bytes 221216 | tf_op jit(solution)/shard_map/ppermute | solution.py:64
  69.0 2.9 %collective-permute-start.8 = (f32[108,128]{1,0:T(8,128)S(1)}, f32[108,128]{1,0:T(8,128)S(1)}, u32[]{:S(2)}, u32[]{:S(2)}) collective-permute-start(f32[108,128]{1,0:T(8,128)S(1)} %get-tuple-element.184), channel_id=1, source_target_pairs={{0,128},{64,192},{128,0},{192,64},{1,129},{65,193},{129,1},{193,65... | collective-permute-start | bytes 165896 | tf_op jit(solution)/shard_map/ppermute | solution.py:64
  76.1 6.2 %collective-permute-start.10 = (f32[108,128]{1,0:T(8,128)S(1)}, f32[108,128]{1,0:T(8,128)S(1)}, u32[]{:S(2)}, u32[]{:S(2)}) collective-permute-start(f32[108,128]{1,0:T(8,128)S(1)} %fusion.37), channel_id=1, source_target_pairs={{0,8},{8,0},{1,9},{9,1},{2,10},{10,2},{3,11},{11,3},{4,12},{12,4},... | collective-permute-start | bytes 165896 | tf_op jit(solution)/shard_map/ppermute | solution.py:91
  84.8 3.8 %collective-permute-start.12 = (f32[108,128]{1,0:T(8,128)S(1)}, f32[108,128]{1,0:T(8,128)S(1)}, u32[]{:S(2)}, u32[]{:S(2)}) collective-permute-start(f32[108,128]{1,0:T(8,128)S(1)} %add.410), channel_id=1, source_target_pairs={{0,128},{64,192},{128,0},{192,64},{1,129},{65,193},{129,1},{193,65... | collective-permute-start | bytes 165896 | tf_op jit(solution)/shard_map/ppermute | solution.py:64
  99.2 3.3 %collective-permute-done.15 = f32[432,128]{1,0:T(8,128)S(1)} collective-permute-done((f32[432,128]{1,0:T(8,128)S(1)}, f32[432,128]{1,0:T(8,128)S(1)}, u32[]{:S(2)}, u32[]{:S(2)}) %collective-permute-start.15) | collective-permute-done | bytes 221216 | tf_op jit(solution)/shard_map/ppermute | solution.py:64
  102.6 2.2 %collective-permute-done.16 = f32[432,128]{1,0:T(8,128)S(1)} collective-permute-done((f32[432,128]{1,0:T(8,128)S(1)}, f32[432,128]{1,0:T(8,128)S(1)}, u32[]{:S(2)}, u32[]{:S(2)}) %collective-permute-start.16) | collective-permute-done | bytes 221216 | tf_op jit(solution)/shard_map/ppermute | solution.py:64
  106.1 2.4 %collective-permute-done.17 = f32[1728,128]{1,0:T(8,128)S(1)} collective-permute-done((f32[1728,128]{1,0:T(8,128)S(1)}, f32[1728,128]{1,0:T(8,128)S(1)}, u32[]{:S(2)}, u32[]{:S(2)}) %collective-permute-start.17) | collective-permute-done | bytes 884768 | tf_op jit(solution)/shard_map/ppermute | solution.py:91
  112.9 4.2 %collective-permute-done.18 = f32[432,128]{1,0:T(8,128)S(1)} collective-permute-done((f32[432,128]{1,0:T(8,128)S(1)}, f32[432,128]{1,0:T(8,128)S(1)}, u32[]{:S(2)}, u32[]{:S(2)}) %collective-permute-start.18) | collective-permute-done | bytes 221216 | tf_op jit(solution)/shard_map/ppermute | solution.py:64
  119.2 3.3 %collective-permute-done.20 = f32[432,128]{1,0:T(8,128)S(1)} collective-permute-done((f32[432,128]{1,0:T(8,128)S(1)}, f32[432,128]{1,0:T(8,128)S(1)}, u32[]{:S(2)}, u32[]{:S(2)}) %collective-permute-start.20) | collective-permute-done | bytes 221216 | tf_op jit(solution)/shard_map/ppermute | solution.py:64
  122.8 2.7 %collective-permute-start.22 = (f32[108,128]{1,0:T(8,128)S(1)}, f32[108,128]{1,0:T(8,128)S(1)}, u32[]{:S(2)}, u32[]{:S(2)}) collective-permute-start(f32[108,128]{1,0:T(8,128)S(1)} %get-tuple-element.181), channel_id=1, source_target_pairs={{0,128},{64,192},{128,0},{192,64},{1,129},{65,193},{129,1},{193,65... | collective-permute-start | bytes 165896 | tf_op jit(solution)/shard_map/ppermute | solution.py:64
  129.7 6.0 %collective-permute-start.24 = (f32[108,128]{1,0:T(8,128)S(1)}, f32[108,128]{1,0:T(8,128)S(1)}, u32[]{:S(2)}, u32[]{:S(2)}) collective-permute-start(f32[108,128]{1,0:T(8,128)S(1)} %fusion.35), channel_id=1, source_target_pairs={{0,8},{8,0},{1,9},{9,1},{2,10},{10,2},{3,11},{11,3},{4,12},{12,4},... | collective-permute-start | bytes 165896 | tf_op jit(solution)/shard_map/ppermute | solution.py:91
  139.3 3.1 %collective-permute-start.26 = (f32[108,128]{1,0:T(8,128)S(1)}, f32[108,128]{1,0:T(8,128)S(1)}, u32[]{:S(2)}, u32[]{:S(2)}) collective-permute-start(f32[108,128]{1,0:T(8,128)S(1)} %add.432), channel_id=1, source_target_pairs={{0,128},{64,192},{128,0},{192,64},{1,129},{65,193},{129,1},{193,65... | collective-permute-start | bytes 165896 | tf_op jit(solution)/shard_map/ppermute | solution.py:64
  153.1 2.5 %collective-permute-done.29 = f32[432,128]{1,0:T(8,128)S(1)} collective-permute-done((f32[432,128]{1,0:T(8,128)S(1)}, f32[432,128]{1,0:T(8,128)S(1)}, u32[]{:S(2)}, u32[]{:S(2)}) %collective-permute-start.29) | collective-permute-done | bytes 221216 | tf_op jit(solution)/shard_map/ppermute | solution.py:64
  155.6 2.2 %collective-permute-done.30 = f32[432,128]{1,0:T(8,128)S(1)} collective-permute-done((f32[432,128]{1,0:T(8,128)S(1)}, f32[432,128]{1,0:T(8,128)S(1)}, u32[]{:S(2)}, u32[]{:S(2)}) %collective-permute-start.30) | collective-permute-done | bytes 221216 | tf_op jit(solution)/shard_map/ppermute | solution.py:64
  159.0 10.6 %collective-permute-start.31 = (f32[128]{0:T(128)S(1)}, f32[128]{0:T(128)S(1)}, u32[]{:S(2)}, u32[]{:S(2)}) collective-permute-start(f32[128]{0:T(128)S(1)} %get-tuple-element.185), channel_id=1, source_target_pairs={{0,3},{1,0},{2,1},{3,2},{4,7},{5,4},{6,5},{7,6},{8,11},{9,8},{10,9... | collective-permute-start | bytes 1544 | tf_op jit(solution)/shard_map/ppermute | solution.py:64
  171.7 2.4 %collective-permute-done.32 = f32[128]{0:T(128)S(1)} collective-permute-done((f32[128]{0:T(128)S(1)}, f32[128]{0:T(128)S(1)}, u32[]{:S(2)}, u32[]{:S(2)}) %collective-permute-start.32) | collective-permute-done | bytes 544 | tf_op jit(solution)/shard_map/ppermute | solution.py:64
  174.2 2.9 %collective-permute-done.33 = f32[128]{0:T(128)S(1)} collective-permute-done((f32[128]{0:T(128)S(1)}, f32[128]{0:T(128)S(1)}, u32[]{:S(2)}, u32[]{:S(2)}) %collective-permute-start.33) | collective-permute-done | bytes 544 | tf_op jit(solution)/shard_map/ppermute | solution.py:64
  (145 shorter events, 72.4 us)
Async XLA Ops:
  14.5 15.9 %collective-permute-start = (bf16[1736,128]{1,0:T(8,128)(2,1)S(1)}, bf16[1736,128]{1,0:T(8,128)(2,1)S(1)}, u32[]{:S(2)}, u32[]{:S(2)}) collective-permute-start(bf16[1736,128]{1,0:T(8,128)(2,1)S(1)} %concatenate.6), channel_id=1, source_target_pairs={{0,1},{1,2},{2,3},{3,0},{4,5},{5,6},{6,7},{7,4},{8,9},{9,10},{10,1... | collective-permute-start | bytes 1333256 | tf_op jit(solution)/shard_map/ppermute | solution.py:64
  16.5 32.1 %collective-permute-start.1 = (bf16[1736,128]{1,0:T(8,128)(2,1)S(1)}, bf16[1736,128]{1,0:T(8,128)(2,1)S(1)}, u32[]{:S(2)}, u32[]{:S(2)}) collective-permute-start(bf16[1736,128]{1,0:T(8,128)(2,1)S(1)} %concatenate.6), channel_id=1, source_target_pairs={{0,2},{1,3},{2,0},{3,1},{4,6},{5,7},{6,4},{7,5},{8,10},{9,11},{10,... | collective-permute-start | bytes 1333256 | tf_op jit(solution)/shard_map/ppermute | solution.py:64
  19.8 28.8 %collective-permute-start.2 = (bf16[1736,128]{1,0:T(8,128)(2,1)S(1)}, bf16[1736,128]{1,0:T(8,128)(2,1)S(1)}, u32[]{:S(2)}, u32[]{:S(2)}) collective-permute-start(bf16[1736,128]{1,0:T(8,128)(2,1)S(1)} %concatenate.6), channel_id=1, source_target_pairs={{0,3},{1,0},{2,1},{3,2},{4,7},{5,4},{6,5},{7,6},{8,11},{9,8},{10,9... | collective-permute-start | bytes 1333256 | tf_op jit(solution)/shard_map/ppermute | solution.py:64
  52.7 8.4 %collective-permute-start.4 = (f32[432,128]{1,0:T(8,128)S(1)}, f32[432,128]{1,0:T(8,128)S(1)}, u32[]{:S(2)}, u32[]{:S(2)}) collective-permute-start(f32[432,128]{1,0:T(8,128)S(1)} %get-tuple-element.176), channel_id=1, source_target_pairs={{0,16},{16,32},{32,48},{48,0},{1,17},{17,33},{33,49},{49,1},{2,18}... | collective-permute-start | bytes 663560 | tf_op jit(solution)/shard_map/ppermute | solution.py:64
  54.3 9.8 %collective-permute-start.5 = (f32[432,128]{1,0:T(8,128)S(1)}, f32[432,128]{1,0:T(8,128)S(1)}, u32[]{:S(2)}, u32[]{:S(2)}) collective-permute-start(f32[432,128]{1,0:T(8,128)S(1)} %get-tuple-element.178), channel_id=1, source_target_pairs={{0,32},{16,48},{32,0},{48,16},{1,33},{17,49},{33,1},{49,17},{2,34}... | collective-permute-start | bytes 663560 | tf_op jit(solution)/shard_map/ppermute | solution.py:64
  55.4 11.6 %collective-permute-start.6 = (f32[432,128]{1,0:T(8,128)S(1)}, f32[432,128]{1,0:T(8,128)S(1)}, u32[]{:S(2)}, u32[]{:S(2)}) collective-permute-start(f32[432,128]{1,0:T(8,128)S(1)} %get-tuple-element.177), channel_id=1, source_target_pairs={{0,48},{16,0},{32,16},{48,32},{1,49},{17,1},{33,17},{49,33},{2,50}... | collective-permute-start | bytes 663560 | tf_op jit(solution)/shard_map/ppermute | solution.py:64
  67.1 6.3 %collective-permute-start.7 = (f32[108,128]{1,0:T(8,128)S(1)}, f32[108,128]{1,0:T(8,128)S(1)}, u32[]{:S(2)}, u32[]{:S(2)}) collective-permute-start(f32[108,128]{1,0:T(8,128)S(1)} %get-tuple-element.182), channel_id=1, source_target_pairs={{0,64},{64,128},{128,192},{192,0},{1,65},{65,129},{129,193},{193,1... | collective-permute-start | bytes 165896 | tf_op jit(solution)/shard_map/ppermute | solution.py:64
  69.0 5.7 %collective-permute-start.8 = (f32[108,128]{1,0:T(8,128)S(1)}, f32[108,128]{1,0:T(8,128)S(1)}, u32[]{:S(2)}, u32[]{:S(2)}) collective-permute-start(f32[108,128]{1,0:T(8,128)S(1)} %get-tuple-element.184), channel_id=1, source_target_pairs={{0,128},{64,192},{128,0},{192,64},{1,129},{65,193},{129,1},{193,65... | collective-permute-start | bytes 165896 | tf_op jit(solution)/shard_map/ppermute | solution.py:64
  76.1 8.3 %collective-permute-start.10 = (f32[108,128]{1,0:T(8,128)S(1)}, f32[108,128]{1,0:T(8,128)S(1)}, u32[]{:S(2)}, u32[]{:S(2)}) collective-permute-start(f32[108,128]{1,0:T(8,128)S(1)} %fusion.37), channel_id=1, source_target_pairs={{0,8},{8,0},{1,9},{9,1},{2,10},{10,2},{3,11},{11,3},{4,12},{12,4},... | collective-permute-start | bytes 165896 | tf_op jit(solution)/shard_map/ppermute | solution.py:91
  84.8 6.5 %collective-permute-start.12 = (f32[108,128]{1,0:T(8,128)S(1)}, f32[108,128]{1,0:T(8,128)S(1)}, u32[]{:S(2)}, u32[]{:S(2)}) collective-permute-start(f32[108,128]{1,0:T(8,128)S(1)} %add.410), channel_id=1, source_target_pairs={{0,128},{64,192},{128,0},{192,64},{1,129},{65,193},{129,1},{193,65... | collective-permute-start | bytes 165896 | tf_op jit(solution)/shard_map/ppermute | solution.py:64
  93.2 6.0 %collective-permute-start.14 = (f32[432,128]{1,0:T(8,128)S(1)}, f32[432,128]{1,0:T(8,128)S(1)}, u32[]{:S(2)}, u32[]{:S(2)}) collective-permute-start(f32[432,128]{1,0:T(8,128)S(1)} %dynamic_update_slice.51), channel_id=1, source_target_pairs={{0,16},{16,32},{32,48},{48,0},{1,17},{17,33},{33,49},{49,1},{2,18}... | collective-permute-start | bytes 663560 | tf_op jit(solution)/shard_map/ppermute | solution.py:64
  94.9 7.6 %collective-permute-start.15 = (f32[432,128]{1,0:T(8,128)S(1)}, f32[432,128]{1,0:T(8,128)S(1)}, u32[]{:S(2)}, u32[]{:S(2)}) collective-permute-start(f32[432,128]{1,0:T(8,128)S(1)} %dynamic_update_slice.51), channel_id=1, source_target_pairs={{0,32},{16,48},{32,0},{48,16},{1,33},{17,49},{33,1},{49,17},{2,34}... | collective-permute-start | bytes 663560 | tf_op jit(solution)/shard_map/ppermute | solution.py:64
  96.5 8.3 %collective-permute-start.16 = (f32[432,128]{1,0:T(8,128)S(1)}, f32[432,128]{1,0:T(8,128)S(1)}, u32[]{:S(2)}, u32[]{:S(2)}) collective-permute-start(f32[432,128]{1,0:T(8,128)S(1)} %dynamic_update_slice.51), channel_id=1, source_target_pairs={{0,48},{16,0},{32,16},{48,32},{1,49},{17,1},{33,17},{49,33},{2,50}... | collective-permute-start | bytes 663560 | tf_op jit(solution)/shard_map/ppermute | solution.py:64
  108.7 8.4 %collective-permute-start.18 = (f32[432,128]{1,0:T(8,128)S(1)}, f32[432,128]{1,0:T(8,128)S(1)}, u32[]{:S(2)}, u32[]{:S(2)}) collective-permute-start(f32[432,128]{1,0:T(8,128)S(1)} %get-tuple-element.173), channel_id=1, source_target_pairs={{0,16},{16,32},{32,48},{48,0},{1,17},{17,33},{33,49},{49,1},{2,18}... | collective-permute-start | bytes 663560 | tf_op jit(solution)/shard_map/ppermute | solution.py:64
  109.4 9.8 %collective-permute-start.19 = (f32[432,128]{1,0:T(8,128)S(1)}, f32[432,128]{1,0:T(8,128)S(1)}, u32[]{:S(2)}, u32[]{:S(2)}) collective-permute-start(f32[432,128]{1,0:T(8,128)S(1)} %get-tuple-element.175), channel_id=1, source_target_pairs={{0,32},{16,48},{32,0},{48,16},{1,33},{17,49},{33,1},{49,17},{2,34}... | collective-permute-start | bytes 663560 | tf_op jit(solution)/shard_map/ppermute | solution.py:64
  110.9 11.6 %collective-permute-start.20 = (f32[432,128]{1,0:T(8,128)S(1)}, f32[432,128]{1,0:T(8,128)S(1)}, u32[]{:S(2)}, u32[]{:S(2)}) collective-permute-start(f32[432,128]{1,0:T(8,128)S(1)} %get-tuple-element.174), channel_id=1, source_target_pairs={{0,48},{16,0},{32,16},{48,32},{1,49},{17,1},{33,17},{49,33},{2,50}... | collective-permute-start | bytes 663560 | tf_op jit(solution)/shard_map/ppermute | solution.py:64
  122.6 6.2 %collective-permute-start.21 = (f32[108,128]{1,0:T(8,128)S(1)}, f32[108,128]{1,0:T(8,128)S(1)}, u32[]{:S(2)}, u32[]{:S(2)}) collective-permute-start(f32[108,128]{1,0:T(8,128)S(1)} %get-tuple-element.179), channel_id=1, source_target_pairs={{0,64},{64,128},{128,192},{192,0},{1,65},{65,129},{129,193},{193,1... | collective-permute-start | bytes 165896 | tf_op jit(solution)/shard_map/ppermute | solution.py:64
  122.8 6.1 %collective-permute-start.22 = (f32[108,128]{1,0:T(8,128)S(1)}, f32[108,128]{1,0:T(8,128)S(1)}, u32[]{:S(2)}, u32[]{:S(2)}) collective-permute-start(f32[108,128]{1,0:T(8,128)S(1)} %get-tuple-element.181), channel_id=1, source_target_pairs={{0,128},{64,192},{128,0},{192,64},{1,129},{65,193},{129,1},{193,65... | collective-permute-start | bytes 165896 | tf_op jit(solution)/shard_map/ppermute | solution.py:64
  129.7 8.2 %collective-permute-start.24 = (f32[108,128]{1,0:T(8,128)S(1)}, f32[108,128]{1,0:T(8,128)S(1)}, u32[]{:S(2)}, u32[]{:S(2)}) collective-permute-start(f32[108,128]{1,0:T(8,128)S(1)} %fusion.35), channel_id=1, source_target_pairs={{0,8},{8,0},{1,9},{9,1},{2,10},{10,2},{3,11},{11,3},{4,12},{12,4},... | collective-permute-start | bytes 165896 | tf_op jit(solution)/shard_map/ppermute | solution.py:91
  139.3 5.9 %collective-permute-start.26 = (f32[108,128]{1,0:T(8,128)S(1)}, f32[108,128]{1,0:T(8,128)S(1)}, u32[]{:S(2)}, u32[]{:S(2)}) collective-permute-start(f32[108,128]{1,0:T(8,128)S(1)} %add.432), channel_id=1, source_target_pairs={{0,128},{64,192},{128,0},{192,64},{1,129},{65,193},{129,1},{193,65... | collective-permute-start | bytes 165896 | tf_op jit(solution)/shard_map/ppermute | solution.py:64
  147.0 6.0 %collective-permute-start.28 = (f32[432,128]{1,0:T(8,128)S(1)}, f32[432,128]{1,0:T(8,128)S(1)}, u32[]{:S(2)}, u32[]{:S(2)}) collective-permute-start(f32[432,128]{1,0:T(8,128)S(1)} %dynamic_update_slice.59), channel_id=1, source_target_pairs={{0,16},{16,32},{32,48},{48,0},{1,17},{17,33},{33,49},{49,1},{2,18}... | collective-permute-start | bytes 663560 | tf_op jit(solution)/shard_map/ppermute | solution.py:64
  148.1 7.5 %collective-permute-start.29 = (f32[432,128]{1,0:T(8,128)S(1)}, f32[432,128]{1,0:T(8,128)S(1)}, u32[]{:S(2)}, u32[]{:S(2)}) collective-permute-start(f32[432,128]{1,0:T(8,128)S(1)} %dynamic_update_slice.59), channel_id=1, source_target_pairs={{0,32},{16,48},{32,0},{48,16},{1,33},{17,49},{33,1},{49,17},{2,34}... | collective-permute-start | bytes 663560 | tf_op jit(solution)/shard_map/ppermute | solution.py:64
  149.8 8.1 %collective-permute-start.30 = (f32[432,128]{1,0:T(8,128)S(1)}, f32[432,128]{1,0:T(8,128)S(1)}, u32[]{:S(2)}, u32[]{:S(2)}) collective-permute-start(f32[432,128]{1,0:T(8,128)S(1)} %dynamic_update_slice.59), channel_id=1, source_target_pairs={{0,48},{16,0},{32,16},{48,32},{1,49},{17,1},{33,17},{49,33},{2,50}... | collective-permute-start | bytes 663560 | tf_op jit(solution)/shard_map/ppermute | solution.py:64
  159.0 12.7 %collective-permute-start.31 = (f32[128]{0:T(128)S(1)}, f32[128]{0:T(128)S(1)}, u32[]{:S(2)}, u32[]{:S(2)}) collective-permute-start(f32[128]{0:T(128)S(1)} %get-tuple-element.185), channel_id=1, source_target_pairs={{0,3},{1,0},{2,1},{3,2},{4,7},{5,4},{6,5},{7,6},{8,11},{9,8},{10,9... | collective-permute-start | bytes 1544 | tf_op jit(solution)/shard_map/ppermute | solution.py:64
  (17 other events, 73.5 us)
where the time goes:
time: 178 us
  waiting for transfers between devices  84.8 us (48%)
  starting transfers between devices  68.7 us (39%)
  matrix products  7.86 us (4%)
  other arithmetic  7.69 us (4%)
  local copies, waits for them, and re-layouts  7.2 us (4%)
    ppermute x30, waiting for transfers between devices, shifted(): lax.ppermute(value, name, [(j, (j + shift) % count) for j in range(count)])  75.6 us
    ppermute x30, starting transfers between devices, shifted(): lax.ppermute(value, name, [(j, (j + shift) % count) for j in range(count)])  56.4 us
    ppermute x4, starting transfers between devices, pair_sum(): return part + lax.ppermute(part, name, [(0, 1), (1, 0)])  12.3 us
    ppermute x4, waiting for transfers between devices, pair_sum(): return part + lax.ppermute(part, name, [(0, 1), (1, 0)])  9.14 us
    select_n x6, other arithmetic, smooth_step(): return jnp.where(degree < counts, updated, field)  4.02 us
  transfers between devices with their start and end apart: 34, of which 31 were waited for; matrix products, arithmetic and copies ran while one was open for 2% of the time, Pallas kernels for 0%

commit v1 on v0

--- a/solution.py
+++ b/solution.py
@@ -49,11 +49,13 @@
         updated = field + diffusion * (beside - 6.0 * field) - discount * field
         return jnp.where(degree < counts, updated, field)
 
-    field = lax.fori_loop(0, MAX_SWEEPS, smooth_step, grid_values)
+    field = grid_values
+    for degree in range(MAX_SWEEPS):
+        field = smooth_step(degree, field)
     matrix = cheb_matrix()
-    field = jnp.einsum("ai,ijlp->ajlp", matrix, field, precision=lax.Precision.HIGHEST)
-    field = jnp.einsum("bj,ajlp->ablp", matrix, field, precision=lax.Precision.HIGHEST)
-    field = jnp.einsum("cl,ablp->abcp", matrix, field, precision=lax.Precision.HIGHEST)
+    field = jnp.einsum("ai,ijlp->ajlp", matrix, field, precision=lax.Precision.HIGH)
+    field = jnp.einsum("bj,ajlp->ablp", matrix, field, precision=lax.Precision.HIGH)
+    field = jnp.einsum("cl,ablp->abcp", matrix, field, precision=lax.Precision.HIGH)
     return field.reshape(GRID * GRID * GRID, -1).astype(jnp.bfloat16)
 
 

time: 178 us -> 176 us (0.989)
  no operation moved by 1% of the time
where the time goes in v1:
time: 176 us
  waiting for transfers between devices  84.7 us (48%)
  starting transfers between devices  68.7 us (39%)
  other arithmetic  8.32 us (5%)
  local copies, waits for them, and re-layouts  6.43 us (4%)
  matrix products  6.31 us (4%)
    ppermute x30, waiting for transfers between devices, shifted(): lax.ppermute(value, name, [(j, (j + shift) % count) for j in range(count)])  75.6 us
    ppermute x30, starting transfers between devices, shifted(): lax.ppermute(value, name, [(j, (j + shift) % count) for j in range(count)])  56.4 us
    ppermute x4, starting transfers between devices, pair_sum(): return part + lax.ppermute(part, name, [(0, 1), (1, 0)])  12.3 us
    ppermute x4, waiting for transfers between devices, pair_sum(): return part + lax.ppermute(part, name, [(0, 1), (1, 0)])  9.14 us
    select_n x6, other arithmetic, smooth_step(): return jnp.where(degree < counts, updated, field)  4.02 us
  transfers between devices with their start and end apart: 34, of which 31 were waited for; matrix products, arithmetic and copies ran while one was open for 2% of the time, Pallas kernels for 0%

profile of v1, /device:TPU:2, one launch (start us, length us, event | category | flops | bytes accessed | tf_op | source)
XLA Modules:
  0.0 175.6 jit_solution(12495108739768013972)
XLA Ops:
  14.7 3.3 %collective-permute-start.1 = (bf16[1736,128]{1,0:T(8,128)(2,1)S(1)}, bf16[1736,128]{1,0:T(8,128)(2,1)S(1)}, u32[]{:S(2)}, u32[]{:S(2)}) collective-permute-start(bf16[1736,128]{1,0:T(8,128)(2,1)S(1)} %concatenate.6), channel_id=1, source_target_pairs={{0,2},{1,3},{2,0},{3,1},{4,6},{5,7},{6,4},{7,5},{8,10},{9,11},{10,... | collective-permute-start | bytes 1333256 | tf_op jit(solution)/shard_map/ppermute | solution.py:66
  18.9 9.6 %collective-permute-done = bf16[1736,128]{1,0:T(8,128)(2,1)S(1)} collective-permute-done((bf16[1736,128]{1,0:T(8,128)(2,1)S(1)}, bf16[1736,128]{1,0:T(8,128)(2,1)S(1)}, u32[]{:S(2)}, u32[]{:S(2)}) %collective-permute-start) | collective-permute-done | bytes 444448 | tf_op jit(solution)/shard_map/ppermute | solution.py:66
  28.6 18.2 %collective-permute-done.1 = bf16[1736,128]{1,0:T(8,128)(2,1)S(1)} collective-permute-done((bf16[1736,128]{1,0:T(8,128)(2,1)S(1)}, bf16[1736,128]{1,0:T(8,128)(2,1)S(1)}, u32[]{:S(2)}, u32[]{:S(2)}) %collective-permute-start.1) | collective-permute-done | bytes 444448 | tf_op jit(solution)/shard_map/ppermute | solution.py:66
  48.2 2.4 %collective-permute-done.3 = f32[1728,128]{1,0:T(8,128)S(1)} collective-permute-done((f32[1728,128]{1,0:T(8,128)S(1)}, f32[1728,128]{1,0:T(8,128)S(1)}, u32[]{:S(2)}, u32[]{:S(2)}) %collective-permute-start.3) | collective-permute-done | bytes 884768 | tf_op jit(solution)/shard_map/ppermute | solution.py:93
  55.9 3.5 %collective-permute-done.4 = f32[432,128]{1,0:T(8,128)S(1)} collective-permute-done((f32[432,128]{1,0:T(8,128)S(1)}, f32[432,128]{1,0:T(8,128)S(1)}, u32[]{:S(2)}, u32[]{:S(2)}) %collective-permute-start.4) | collective-permute-done | bytes 221216 | tf_op jit(solution)/shard_map/ppermute | solution.py:66
  59.4 3.0 %collective-permute-done.5 = f32[432,128]{1,0:T(8,128)S(1)} collective-permute-done((f32[432,128]{1,0:T(8,128)S(1)}, f32[432,128]{1,0:T(8,128)S(1)}, u32[]{:S(2)}, u32[]{:S(2)}) %collective-permute-start.5) | collective-permute-done | bytes 221216 | tf_op jit(solution)/shard_map/ppermute | solution.py:66
  62.4 3.0 %collective-permute-done.6 = f32[432,128]{1,0:T(8,128)S(1)} collective-permute-done((f32[432,128]{1,0:T(8,128)S(1)}, f32[432,128]{1,0:T(8,128)S(1)}, u32[]{:S(2)}, u32[]{:S(2)}) %collective-permute-start.6) | collective-permute-done | bytes 221216 | tf_op jit(solution)/shard_map/ppermute | solution.py:66
  67.1 2.9 %collective-permute-start.8 = (f32[108,128]{1,0:T(8,128)S(1)}, f32[108,128]{1,0:T(8,128)S(1)}, u32[]{:S(2)}, u32[]{:S(2)}) collective-permute-start(f32[108,128]{1,0:T(8,128)S(1)} %get-tuple-element.41), channel_id=1, source_target_pairs={{0,128},{64,192},{128,0},{192,64},{1,129},{65,193},{129,1},{193,65... | collective-permute-start | bytes 165896 | tf_op jit(solution)/shard_map/ppermute | solution.py:66
  74.2 6.2 %collective-permute-start.10 = (f32[108,128]{1,0:T(8,128)S(1)}, f32[108,128]{1,0:T(8,128)S(1)}, u32[]{:S(2)}, u32[]{:S(2)}) collective-permute-start(f32[108,128]{1,0:T(8,128)S(1)} %fusion.87), channel_id=1, source_target_pairs={{0,8},{8,0},{1,9},{9,1},{2,10},{10,2},{3,11},{11,3},{4,12},{12,4},... | collective-permute-start | bytes 165896 | tf_op jit(solution)/shard_map/ppermute | solution.py:93
  82.9 3.8 %collective-permute-start.12 = (f32[108,128]{1,0:T(8,128)S(1)}, f32[108,128]{1,0:T(8,128)S(1)}, u32[]{:S(2)}, u32[]{:S(2)}) collective-permute-start(f32[108,128]{1,0:T(8,128)S(1)} %add.484), channel_id=1, source_target_pairs={{0,128},{64,192},{128,0},{192,64},{1,129},{65,193},{129,1},{193,65... | collective-permute-start | bytes 165896 | tf_op jit(solution)/shard_map/ppermute | solution.py:66
  97.4 3.3 %collective-permute-done.15 = f32[432,128]{1,0:T(8,128)S(1)} collective-permute-done((f32[432,128]{1,0:T(8,128)S(1)}, f32[432,128]{1,0:T(8,128)S(1)}, u32[]{:S(2)}, u32[]{:S(2)}) %collective-permute-start.15) | collective-permute-done | bytes 221216 | tf_op jit(solution)/shard_map/ppermute | solution.py:66
  100.7 2.2 %collective-permute-done.16 = f32[432,128]{1,0:T(8,128)S(1)} collective-permute-done((f32[432,128]{1,0:T(8,128)S(1)}, f32[432,128]{1,0:T(8,128)S(1)}, u32[]{:S(2)}, u32[]{:S(2)}) %collective-permute-start.16) | collective-permute-done | bytes 221216 | tf_op jit(solution)/shard_map/ppermute | solution.py:66
  104.2 2.4 %collective-permute-done.17 = f32[1728,128]{1,0:T(8,128)S(1)} collective-permute-done((f32[1728,128]{1,0:T(8,128)S(1)}, f32[1728,128]{1,0:T(8,128)S(1)}, u32[]{:S(2)}, u32[]{:S(2)}) %collective-permute-start.17) | collective-permute-done | bytes 884768 | tf_op jit(solution)/shard_map/ppermute | solution.py:93
  111.0 4.2 %collective-permute-done.18 = f32[432,128]{1,0:T(8,128)S(1)} collective-permute-done((f32[432,128]{1,0:T(8,128)S(1)}, f32[432,128]{1,0:T(8,128)S(1)}, u32[]{:S(2)}, u32[]{:S(2)}) %collective-permute-start.18) | collective-permute-done | bytes 221216 | tf_op jit(solution)/shard_map/ppermute | solution.py:66
  115.2 2.2 %collective-permute-done.19 = f32[432,128]{1,0:T(8,128)S(1)} collective-permute-done((f32[432,128]{1,0:T(8,128)S(1)}, f32[432,128]{1,0:T(8,128)S(1)}, u32[]{:S(2)}, u32[]{:S(2)}) %collective-permute-start.19) | collective-permute-done | bytes 221216 | tf_op jit(solution)/shard_map/ppermute | solution.py:66
  117.4 3.3 %collective-permute-done.20 = f32[432,128]{1,0:T(8,128)S(1)} collective-permute-done((f32[432,128]{1,0:T(8,128)S(1)}, f32[432,128]{1,0:T(8,128)S(1)}, u32[]{:S(2)}, u32[]{:S(2)}) %collective-permute-start.20) | collective-permute-done | bytes 221216 | tf_op jit(solution)/shard_map/ppermute | solution.py:66
  120.9 2.7 %collective-permute-start.22 = (f32[108,128]{1,0:T(8,128)S(1)}, f32[108,128]{1,0:T(8,128)S(1)}, u32[]{:S(2)}, u32[]{:S(2)}) collective-permute-start(f32[108,128]{1,0:T(8,128)S(1)} %get-tuple-element.38), channel_id=1, source_target_pairs={{0,128},{64,192},{128,0},{192,64},{1,129},{65,193},{129,1},{193,65... | collective-permute-start | bytes 165896 | tf_op jit(solution)/shard_map/ppermute | solution.py:66
  127.8 6.0 %collective-permute-start.24 = (f32[108,128]{1,0:T(8,128)S(1)}, f32[108,128]{1,0:T(8,128)S(1)}, u32[]{:S(2)}, u32[]{:S(2)}) collective-permute-start(f32[108,128]{1,0:T(8,128)S(1)} %fusion.85), channel_id=1, source_target_pairs={{0,8},{8,0},{1,9},{9,1},{2,10},{10,2},{3,11},{11,3},{4,12},{12,4},... | collective-permute-start | bytes 165896 | tf_op jit(solution)/shard_map/ppermute | solution.py:93
  137.4 3.1 %collective-permute-start.26 = (f32[108,128]{1,0:T(8,128)S(1)}, f32[108,128]{1,0:T(8,128)S(1)}, u32[]{:S(2)}, u32[]{:S(2)}) collective-permute-start(f32[108,128]{1,0:T(8,128)S(1)} %add.506), channel_id=1, source_target_pairs={{0,128},{64,192},{128,0},{192,64},{1,129},{65,193},{129,1},{193,65... | collective-permute-start | bytes 165896 | tf_op jit(solution)/shard_map/ppermute | solution.py:66
  151.3 2.4 %collective-permute-done.29 = f32[432,128]{1,0:T(8,128)S(1)} collective-permute-done((f32[432,128]{1,0:T(8,128)S(1)}, f32[432,128]{1,0:T(8,128)S(1)}, u32[]{:S(2)}, u32[]{:S(2)}) %collective-permute-start.29) | collective-permute-done | bytes 221216 | tf_op jit(solution)/shard_map/ppermute | solution.py:66
  153.7 2.2 %collective-permute-done.30 = f32[432,128]{1,0:T(8,128)S(1)} collective-permute-done((f32[432,128]{1,0:T(8,128)S(1)}, f32[432,128]{1,0:T(8,128)S(1)}, u32[]{:S(2)}, u32[]{:S(2)}) %collective-permute-start.30) | collective-permute-done | bytes 221216 | tf_op jit(solution)/shard_map/ppermute | solution.py:66
  157.1 10.7 %collective-permute-start.31 = (f32[128]{0:T(128)S(1)}, f32[128]{0:T(128)S(1)}, u32[]{:S(2)}, u32[]{:S(2)}) collective-permute-start(f32[128]{0:T(128)S(1)} %get-tuple-element.42), channel_id=1, source_target_pairs={{0,3},{1,0},{2,1},{3,2},{4,7},{5,4},{6,5},{7,6},{8,11},{9,8},{10,9... | collective-permute-start | bytes 1544 | tf_op jit(solution)/shard_map/ppermute | solution.py:66
  169.8 2.4 %collective-permute-done.32 = f32[128]{0:T(128)S(1)} collective-permute-done((f32[128]{0:T(128)S(1)}, f32[128]{0:T(128)S(1)}, u32[]{:S(2)}, u32[]{:S(2)}) %collective-permute-start.32) | collective-permute-done | bytes 544 | tf_op jit(solution)/shard_map/ppermute | solution.py:66
  172.3 2.9 %collective-permute-done.33 = f32[128]{0:T(128)S(1)} collective-permute-done((f32[128]{0:T(128)S(1)}, f32[128]{0:T(128)S(1)}, u32[]{:S(2)}, u32[]{:S(2)}) %collective-permute-start.33) | collective-permute-done | bytes 544 | tf_op jit(solution)/shard_map/ppermute | solution.py:66
  (131 shorter events, 68.6 us)
Async XLA Ops:
  12.7 15.9 %collective-permute-start = (bf16[1736,128]{1,0:T(8,128)(2,1)S(1)}, bf16[1736,128]{1,0:T(8,128)(2,1)S(1)}, u32[]{:S(2)}, u32[]{:S(2)}) collective-permute-start(bf16[1736,128]{1,0:T(8,128)(2,1)S(1)} %concatenate.6), channel_id=1, source_target_pairs={{0,1},{1,2},{2,3},{3,0},{4,5},{5,6},{6,7},{7,4},{8,9},{9,10},{10,1... | collective-permute-start | bytes 1333256 | tf_op jit(solution)/shard_map/ppermute | solution.py:66
  14.7 32.1 %collective-permute-start.1 = (bf16[1736,128]{1,0:T(8,128)(2,1)S(1)}, bf16[1736,128]{1,0:T(8,128)(2,1)S(1)}, u32[]{:S(2)}, u32[]{:S(2)}) collective-permute-start(bf16[1736,128]{1,0:T(8,128)(2,1)S(1)} %concatenate.6), channel_id=1, source_target_pairs={{0,2},{1,3},{2,0},{3,1},{4,6},{5,7},{6,4},{7,5},{8,10},{9,11},{10,... | collective-permute-start | bytes 1333256 | tf_op jit(solution)/shard_map/ppermute | solution.py:66
  17.9 28.8 %collective-permute-start.2 = (bf16[1736,128]{1,0:T(8,128)(2,1)S(1)}, bf16[1736,128]{1,0:T(8,128)(2,1)S(1)}, u32[]{:S(2)}, u32[]{:S(2)}) collective-permute-start(bf16[1736,128]{1,0:T(8,128)(2,1)S(1)} %concatenate.6), channel_id=1, source_target_pairs={{0,3},{1,0},{2,1},{3,2},{4,7},{5,4},{6,5},{7,6},{8,11},{9,8},{10,9... | collective-permute-start | bytes 1333256 | tf_op jit(solution)/shard_map/ppermute | solution.py:66
  50.8 8.6 %collective-permute-start.4 = (f32[432,128]{1,0:T(8,128)S(1)}, f32[432,128]{1,0:T(8,128)S(1)}, u32[]{:S(2)}, u32[]{:S(2)}) collective-permute-start(f32[432,128]{1,0:T(8,128)S(1)} %get-tuple-element.33), channel_id=1, source_target_pairs={{0,16},{16,32},{32,48},{48,0},{1,17},{17,33},{33,49},{49,1},{2,18}... | collective-permute-start | bytes 663560 | tf_op jit(solution)/shard_map/ppermute | solution.py:66
  52.6 9.8 %collective-permute-start.5 = (f32[432,128]{1,0:T(8,128)S(1)}, f32[432,128]{1,0:T(8,128)S(1)}, u32[]{:S(2)}, u32[]{:S(2)}) collective-permute-start(f32[432,128]{1,0:T(8,128)S(1)} %get-tuple-element.35), channel_id=1, source_target_pairs={{0,32},{16,48},{32,0},{48,16},{1,33},{17,49},{33,1},{49,17},{2,34}... | collective-permute-start | bytes 663560 | tf_op jit(solution)/shard_map/ppermute | solution.py:66
  53.7 11.6 %collective-permute-start.6 = (f32[432,128]{1,0:T(8,128)S(1)}, f32[432,128]{1,0:T(8,128)S(1)}, u32[]{:S(2)}, u32[]{:S(2)}) collective-permute-start(f32[432,128]{1,0:T(8,128)S(1)} %get-tuple-element.34), channel_id=1, source_target_pairs={{0,48},{16,0},{32,16},{48,32},{1,49},{17,1},{33,17},{49,33},{2,50}... | collective-permute-start | bytes 663560 | tf_op jit(solution)/shard_map/ppermute | solution.py:66
  65.5 6.1 %collective-permute-start.7 = (f32[108,128]{1,0:T(8,128)S(1)}, f32[108,128]{1,0:T(8,128)S(1)}, u32[]{:S(2)}, u32[]{:S(2)}) collective-permute-start(f32[108,128]{1,0:T(8,128)S(1)} %get-tuple-element.39), channel_id=1, source_target_pairs={{0,64},{64,128},{128,192},{192,0},{1,65},{65,129},{129,193},{193,1... | collective-permute-start | bytes 165896 | tf_op jit(solution)/shard_map/ppermute | solution.py:66
  67.1 5.7 %collective-permute-start.8 = (f32[108,128]{1,0:T(8,128)S(1)}, f32[108,128]{1,0:T(8,128)S(1)}, u32[]{:S(2)}, u32[]{:S(2)}) collective-permute-start(f32[108,128]{1,0:T(8,128)S(1)} %get-tuple-element.41), channel_id=1, source_target_pairs={{0,128},{64,192},{128,0},{192,64},{1,129},{65,193},{129,1},{193,65... | collective-permute-start | bytes 165896 | tf_op jit(solution)/shard_map/ppermute | solution.py:66
  74.2 8.4 %collective-permute-start.10 = (f32[108,128]{1,0:T(8,128)S(1)}, f32[108,128]{1,0:T(8,128)S(1)}, u32[]{:S(2)}, u32[]{:S(2)}) collective-permute-start(f32[108,128]{1,0:T(8,128)S(1)} %fusion.87), channel_id=1, source_target_pairs={{0,8},{8,0},{1,9},{9,1},{2,10},{10,2},{3,11},{11,3},{4,12},{12,4},... | collective-permute-start | bytes 165896 | tf_op jit(solution)/shard_map/ppermute | solution.py:93
  82.9 6.6 %collective-permute-start.12 = (f32[108,128]{1,0:T(8,128)S(1)}, f32[108,128]{1,0:T(8,128)S(1)}, u32[]{:S(2)}, u32[]{:S(2)}) collective-permute-start(f32[108,128]{1,0:T(8,128)S(1)} %add.484), channel_id=1, source_target_pairs={{0,128},{64,192},{128,0},{192,64},{1,129},{65,193},{129,1},{193,65... | collective-permute-start | bytes 165896 | tf_op jit(solution)/shard_map/ppermute | solution.py:66
  91.3 6.0 %collective-permute-start.14 = (f32[432,128]{1,0:T(8,128)S(1)}, f32[432,128]{1,0:T(8,128)S(1)}, u32[]{:S(2)}, u32[]{:S(2)}) collective-permute-start(f32[432,128]{1,0:T(8,128)S(1)} %dynamic_update_slice.51), channel_id=1, source_target_pairs={{0,16},{16,32},{32,48},{48,0},{1,17},{17,33},{33,49},{49,1},{2,18}... | collective-permute-start | bytes 663560 | tf_op jit(solution)/shard_map/ppermute | solution.py:66
  93.0 7.6 %collective-permute-start.15 = (f32[432,128]{1,0:T(8,128)S(1)}, f32[432,128]{1,0:T(8,128)S(1)}, u32[]{:S(2)}, u32[]{:S(2)}) collective-permute-start(f32[432,128]{1,0:T(8,128)S(1)} %dynamic_update_slice.51), channel_id=1, source_target_pairs={{0,32},{16,48},{32,0},{48,16},{1,33},{17,49},{33,1},{49,17},{2,34}... | collective-permute-start | bytes 663560 | tf_op jit(solution)/shard_map/ppermute | solution.py:66
  94.6 8.3 %collective-permute-start.16 = (f32[432,128]{1,0:T(8,128)S(1)}, f32[432,128]{1,0:T(8,128)S(1)}, u32[]{:S(2)}, u32[]{:S(2)}) collective-permute-start(f32[432,128]{1,0:T(8,128)S(1)} %dynamic_update_slice.51), channel_id=1, source_target_pairs={{0,48},{16,0},{32,16},{48,32},{1,49},{17,1},{33,17},{49,33},{2,50}... | collective-permute-start | bytes 663560 | tf_op jit(solution)/shard_map/ppermute | solution.py:66
  106.8 8.4 %collective-permute-start.18 = (f32[432,128]{1,0:T(8,128)S(1)}, f32[432,128]{1,0:T(8,128)S(1)}, u32[]{:S(2)}, u32[]{:S(2)}) collective-permute-start(f32[432,128]{1,0:T(8,128)S(1)} %get-tuple-element.30), channel_id=1, source_target_pairs={{0,16},{16,32},{32,48},{48,0},{1,17},{17,33},{33,49},{49,1},{2,18}... | collective-permute-start | bytes 663560 | tf_op jit(solution)/shard_map/ppermute | solution.py:66
  107.5 9.8 %collective-permute-start.19 = (f32[432,128]{1,0:T(8,128)S(1)}, f32[432,128]{1,0:T(8,128)S(1)}, u32[]{:S(2)}, u32[]{:S(2)}) collective-permute-start(f32[432,128]{1,0:T(8,128)S(1)} %get-tuple-element.32), channel_id=1, source_target_pairs={{0,32},{16,48},{32,0},{48,16},{1,33},{17,49},{33,1},{49,17},{2,34}... | collective-permute-start | bytes 663560 | tf_op jit(solution)/shard_map/ppermute | solution.py:66
  109.0 11.7 %collective-permute-start.20 = (f32[432,128]{1,0:T(8,128)S(1)}, f32[432,128]{1,0:T(8,128)S(1)}, u32[]{:S(2)}, u32[]{:S(2)}) collective-permute-start(f32[432,128]{1,0:T(8,128)S(1)} %get-tuple-element.31), channel_id=1, source_target_pairs={{0,48},{16,0},{32,16},{48,32},{1,49},{17,1},{33,17},{49,33},{2,50}... | collective-permute-start | bytes 663560 | tf_op jit(solution)/shard_map/ppermute | solution.py:66
  120.8 6.1 %collective-permute-start.21 = (f32[108,128]{1,0:T(8,128)S(1)}, f32[108,128]{1,0:T(8,128)S(1)}, u32[]{:S(2)}, u32[]{:S(2)}) collective-permute-start(f32[108,128]{1,0:T(8,128)S(1)} %get-tuple-element.36), channel_id=1, source_target_pairs={{0,64},{64,128},{128,192},{192,0},{1,65},{65,129},{129,193},{193,1... | collective-permute-start | bytes 165896 | tf_op jit(solution)/shard_map/ppermute | solution.py:66
  120.9 5.9 %collective-permute-start.22 = (f32[108,128]{1,0:T(8,128)S(1)}, f32[108,128]{1,0:T(8,128)S(1)}, u32[]{:S(2)}, u32[]{:S(2)}) collective-permute-start(f32[108,128]{1,0:T(8,128)S(1)} %get-tuple-element.38), channel_id=1, source_target_pairs={{0,128},{64,192},{128,0},{192,64},{1,129},{65,193},{129,1},{193,65... | collective-permute-start | bytes 165896 | tf_op jit(solution)/shard_map/ppermute | solution.py:66
  127.8 8.2 %collective-permute-start.24 = (f32[108,128]{1,0:T(8,128)S(1)}, f32[108,128]{1,0:T(8,128)S(1)}, u32[]{:S(2)}, u32[]{:S(2)}) collective-permute-start(f32[108,128]{1,0:T(8,128)S(1)} %fusion.85), channel_id=1, source_target_pairs={{0,8},{8,0},{1,9},{9,1},{2,10},{10,2},{3,11},{11,3},{4,12},{12,4},... | collective-permute-start | bytes 165896 | tf_op jit(solution)/shard_map/ppermute | solution.py:93
  137.4 5.9 %collective-permute-start.26 = (f32[108,128]{1,0:T(8,128)S(1)}, f32[108,128]{1,0:T(8,128)S(1)}, u32[]{:S(2)}, u32[]{:S(2)}) collective-permute-start(f32[108,128]{1,0:T(8,128)S(1)} %add.506), channel_id=1, source_target_pairs={{0,128},{64,192},{128,0},{192,64},{1,129},{65,193},{129,1},{193,65... | collective-permute-start | bytes 165896 | tf_op jit(solution)/shard_map/ppermute | solution.py:66
  145.2 6.1 %collective-permute-start.28 = (f32[432,128]{1,0:T(8,128)S(1)}, f32[432,128]{1,0:T(8,128)S(1)}, u32[]{:S(2)}, u32[]{:S(2)}) collective-permute-start(f32[432,128]{1,0:T(8,128)S(1)} %dynamic_update_slice.59), channel_id=1, source_target_pairs={{0,16},{16,32},{32,48},{48,0},{1,17},{17,33},{33,49},{49,1},{2,18}... | collective-permute-start | bytes 663560 | tf_op jit(solution)/shard_map/ppermute | solution.py:66
  146.2 7.5 %collective-permute-start.29 = (f32[432,128]{1,0:T(8,128)S(1)}, f32[432,128]{1,0:T(8,128)S(1)}, u32[]{:S(2)}, u32[]{:S(2)}) collective-permute-start(f32[432,128]{1,0:T(8,128)S(1)} %dynamic_update_slice.59), channel_id=1, source_target_pairs={{0,32},{16,48},{32,0},{48,16},{1,33},{17,49},{33,1},{49,17},{2,34}... | collective-permute-start | bytes 663560 | tf_op jit(solution)/shard_map/ppermute | solution.py:66
  147.9 8.1 %collective-permute-start.30 = (f32[432,128]{1,0:T(8,128)S(1)}, f32[432,128]{1,0:T(8,128)S(1)}, u32[]{:S(2)}, u32[]{:S(2)}) collective-permute-start(f32[432,128]{1,0:T(8,128)S(1)} %dynamic_update_slice.59), channel_id=1, source_target_pairs={{0,48},{16,0},{32,16},{48,32},{1,49},{17,1},{33,17},{49,33},{2,50}... | collective-permute-start | bytes 663560 | tf_op jit(solution)/shard_map/ppermute | solution.py:66
  157.1 12.7 %collective-permute-start.31 = (f32[128]{0:T(128)S(1)}, f32[128]{0:T(128)S(1)}, u32[]{:S(2)}, u32[]{:S(2)}) collective-permute-start(f32[128]{0:T(128)S(1)} %get-tuple-element.42), channel_id=1, source_target_pairs={{0,3},{1,0},{2,1},{3,2},{4,7},{5,4},{6,5},{7,6},{8,11},{9,8},{10,9... | collective-permute-start | bytes 1544 | tf_op jit(solution)/shard_map/ppermute | solution.py:66
  (16 other events, 68.6 us)

commit v2 on v1

--- a/solution.py
+++ b/solution.py
@@ -49,9 +49,7 @@
         updated = field + diffusion * (beside - 6.0 * field) - discount * field
         return jnp.where(degree < counts, updated, field)
 
-    field = grid_values
-    for degree in range(MAX_SWEEPS):
-        field = smooth_step(degree, field)
+    field = lax.fori_loop(0, MAX_SWEEPS, smooth_step, grid_values)
     matrix = cheb_matrix()
     field = jnp.einsum("ai,ijlp->ajlp", matrix, field, precision=lax.Precision.HIGH)
     field = jnp.einsum("bj,ajlp->ablp", matrix, field, precision=lax.Precision.HIGH)
@@ -94,12 +92,13 @@
 
 
 def scen_sum(part):
-    part = pair_sum(part, "core")
+    part = axis_scatter_sum(part, "core")
     part = axis_scatter_sum(part, "x")
     part = axis_scatter_sum(part, "y")
     part = pair_sum(part, "zh")
     part = axis_gather(part, "y")
-    return axis_gather(part, "x")
+    part = axis_gather(part, "x")
+    return axis_gather(part, "core")
 
 
 def shards(

time: 176 us -> 161 us (0.915)
  waiting for transfers between devices: 84.7 us -> 70 us
    ppermute x30 -> x34, waiting for transfers between devices: 75.6 us -> 66.4 us  [shifted(): lax.ppermute(value, name, [(j, (j + shift) % count) for j in range(count)])]
    ppermute x4 -> x2, waiting for transfers between devices: 9.14 us -> 3.57 us  [pair_sum(): return part + lax.ppermute(part, name, [(0, 1), (1, 0)])]
    ppermute x30 -> x34, starting transfers between devices: 56.4 us -> 56.1 us  [shifted(): lax.ppermute(value, name, [(j, (j + shift) % count) for j in range(count)])]
    ppermute x4 -> x2, starting transfers between devices: 12.3 us -> 12.2 us  [pair_sum(): return part + lax.ppermute(part, name, [(0, 1), (1, 0)])]
  transfers between devices with their start and end apart: 34 -> 36, of which waited for: 31 -> 34; matrix products, arithmetic and copies ran while one was open for 2% -> 2% of each run, Pallas kernels for 0% -> 0%
where the time goes in v2:
time: 161 us; the launch traced here: 160 us
  waiting for transfers between devices  70 us (43%)
  starting transfers between devices  68.3 us (42%)
  other arithmetic  7.54 us (5%)
  local copies, waits for them, and re-layouts  6.66 us (4%)
  matrix products  6.32 us (4%)
    ppermute x34, waiting for transfers between devices, shifted(): lax.ppermute(value, name, [(j, (j + shift) % count) for j in range(count)])  66.4 us
    ppermute x34, starting transfers between devices, shifted(): lax.ppermute(value, name, [(j, (j + shift) % count) for j in range(count)])  56.1 us
    ppermute x2, starting transfers between devices, pair_sum(): return part + lax.ppermute(part, name, [(0, 1), (1, 0)])  12.2 us
    select_n x6, other arithmetic, smooth_step(): return jnp.where(degree < counts, updated, field)  4.02 us
    ppermute x2, waiting for transfers between devices, pair_sum(): return part + lax.ppermute(part, name, [(0, 1), (1, 0)])  3.57 us
  transfers between devices with their start and end apart: 36, of which 34 were waited for; matrix products, arithmetic and copies ran while one was open for 2% of the time, Pallas kernels for 0%

profile of v2, /device:TPU:2, one launch (start us, length us, event | category | flops | bytes accessed | tf_op | source)
XLA Modules:
  0.0 160.4 jit_solution(10566624588410695114)
XLA Ops:
  4.3 5.0 %while.15 = (s32[]{:T(128)}, f32[12,12,12,128]{3,2,1,0:T(8,128)S(1)}, s32[128]{0:T(128)S(1)}, f32[128]{0:T(128)S(1)}, f32[128]{0:T(128)S(1)}, /*index=5*/s32[]{:T(128)}) while((s32[]{:T(128)}, f32[12,12,12,128]{3,2,1,0:T(8,128)S(1)}, s32[128]{0:T(128)S(1)}, f32[128]{0:T(128)S(1)}, f32[128]{0:T(128)S(1)}, /*index=5*/s32[]{:T(128)}) %tuple.94), condition=%wide.region_5.6_spmd, body=%wide.region_4.5_spmd.sunk | while | flops 2654338 | bytes 3540809 | solution.py:52
  13.0 2.0 %collective-permute-start = (bf16[1736,128]{1,0:T(8,128)(2,1)S(1)}, bf16[1736,128]{1,0:T(8,128)(2,1)S(1)}, u32[]{:S(2)}, u32[]{:S(2)}) collective-permute-start(bf16[1736,128]{1,0:T(8,128)(2,1)S(1)} %concatenate.6), channel_id=1, source_target_pairs={{0,1},{1,2},{2,3},{3,0},{4,5},{5,6},{6,7},{7,4},{8,9},{9,10},{10,1... | collective-permute-start | bytes 1333256 | tf_op jit(solution)/shard_map/ppermute | solution.py:64
  15.0 3.3 %collective-permute-start.1 = (bf16[1736,128]{1,0:T(8,128)(2,1)S(1)}, bf16[1736,128]{1,0:T(8,128)(2,1)S(1)}, u32[]{:S(2)}, u32[]{:S(2)}) collective-permute-start(bf16[1736,128]{1,0:T(8,128)(2,1)S(1)} %concatenate.6), channel_id=1, source_target_pairs={{0,2},{1,3},{2,0},{3,1},{4,6},{5,7},{6,4},{7,5},{8,10},{9,11},{10,... | collective-permute-start | bytes 1333256 | tf_op jit(solution)/shard_map/ppermute | solution.py:64
  19.3 9.6 %collective-permute-done = bf16[1736,128]{1,0:T(8,128)(2,1)S(1)} collective-permute-done((bf16[1736,128]{1,0:T(8,128)(2,1)S(1)}, bf16[1736,128]{1,0:T(8,128)(2,1)S(1)}, u32[]{:S(2)}, u32[]{:S(2)}) %collective-permute-start) | collective-permute-done | bytes 444448 | tf_op jit(solution)/shard_map/ppermute | solution.py:64
  28.9 18.2 %collective-permute-done.1 = bf16[1736,128]{1,0:T(8,128)(2,1)S(1)} collective-permute-done((bf16[1736,128]{1,0:T(8,128)(2,1)S(1)}, bf16[1736,128]{1,0:T(8,128)(2,1)S(1)}, u32[]{:S(2)}, u32[]{:S(2)}) %collective-permute-start.1) | collective-permute-done | bytes 444448 | tf_op jit(solution)/shard_map/ppermute | solution.py:64
  48.7 1.7 %collective-permute-done.3 = f32[864,128]{1,0:T(8,128)S(1)} collective-permute-done((f32[864,128]{1,0:T(8,128)S(1)}, f32[864,128]{1,0:T(8,128)S(1)}, u32[]{:S(2)}, u32[]{:S(2)}) %collective-permute-start.3) | collective-permute-done | bytes 442400 | tf_op jit(solution)/shard_map/ppermute | solution.py:64
  53.3 2.2 %collective-permute-start.6 = (f32[216,128]{1,0:T(8,128)S(1)}, f32[216,128]{1,0:T(8,128)S(1)}, u32[]{:S(2)}, u32[]{:S(2)}) collective-permute-start(f32[216,128]{1,0:T(8,128)S(1)} %get-tuple-element.177), channel_id=1, source_target_pairs={{0,48},{16,0},{32,16},{48,32},{1,49},{17,1},{33,17},{49,33},{2,50}... | collective-permute-start | bytes 331784 | tf_op jit(solution)/shard_map/ppermute | solution.py:64
  55.8 3.8 %collective-permute-done.5 = f32[216,128]{1,0:T(8,128)S(1)} collective-permute-done((f32[216,128]{1,0:T(8,128)S(1)}, f32[216,128]{1,0:T(8,128)S(1)}, u32[]{:S(2)}, u32[]{:S(2)}) %collective-permute-start.5) | collective-permute-done | bytes 110624 | tf_op jit(solution)/shard_map/ppermute | solution.py:64
  61.9 2.9 %collective-permute-start.8 = (f32[54,128]{1,0:T(8,128)S(1)}, f32[54,128]{1,0:T(8,128)S(1)}, u32[]{:S(2)}, u32[]{:S(2)}) collective-permute-start(f32[54,128]{1,0:T(8,128)S(1)} %get-tuple-element.184), channel_id=1, source_target_pairs={{0,128},{64,192},{128,0},{192,64},{1,129},{65,193},{129,1},{193,65... | collective-permute-start | bytes 82952 | tf_op jit(solution)/shard_map/ppermute | solution.py:64
  68.7 6.2 %collective-permute-start.10 = (f32[54,128]{1,0:T(8,128)S(1)}, f32[54,128]{1,0:T(8,128)S(1)}, u32[]{:S(2)}, u32[]{:S(2)}) collective-permute-start(f32[54,128]{1,0:T(8,128)S(1)} %fusion.39), channel_id=1, source_target_pairs={{0,8},{8,0},{1,9},{9,1},{2,10},{10,2},{3,11},{11,3},{4,12},{12,4},... | collective-permute-start | bytes 82952 | tf_op jit(solution)/shard_map/ppermute | solution.py:91
  76.9 3.8 %collective-permute-start.12 = (f32[54,128]{1,0:T(8,128)S(1)}, f32[54,128]{1,0:T(8,128)S(1)}, u32[]{:S(2)}, u32[]{:S(2)}) collective-permute-start(f32[54,128]{1,0:T(8,128)S(1)} %add.444), channel_id=1, source_target_pairs={{0,128},{64,192},{128,0},{192,64},{1,129},{65,193},{129,1},{193,65... | collective-permute-start | bytes 82952 | tf_op jit(solution)/shard_map/ppermute | solution.py:64
  89.9 2.9 %collective-permute-done.15 = f32[216,128]{1,0:T(8,128)S(1)} collective-permute-done((f32[216,128]{1,0:T(8,128)S(1)}, f32[216,128]{1,0:T(8,128)S(1)}, u32[]{:S(2)}, u32[]{:S(2)}) %collective-permute-start.15) | collective-permute-done | bytes 110624 | tf_op jit(solution)/shard_map/ppermute | solution.py:64
  99.7 1.9 %collective-permute-start.20 = (f32[216,128]{1,0:T(8,128)S(1)}, f32[216,128]{1,0:T(8,128)S(1)}, u32[]{:S(2)}, u32[]{:S(2)}) collective-permute-start(f32[216,128]{1,0:T(8,128)S(1)} %get-tuple-element.175), channel_id=1, source_target_pairs={{0,32},{16,48},{32,0},{48,16},{1,33},{17,49},{33,1},{49,17},{2,34}... | collective-permute-start | bytes 331784 | tf_op jit(solution)/shard_map/ppermute | solution.py:64
  101.6 2.2 %collective-permute-start.21 = (f32[216,128]{1,0:T(8,128)S(1)}, f32[216,128]{1,0:T(8,128)S(1)}, u32[]{:S(2)}, u32[]{:S(2)}) collective-permute-start(f32[216,128]{1,0:T(8,128)S(1)} %get-tuple-element.174), channel_id=1, source_target_pairs={{0,48},{16,0},{32,16},{48,32},{1,49},{17,1},{33,17},{49,33},{2,50}... | collective-permute-start | bytes 331784 | tf_op jit(solution)/shard_map/ppermute | solution.py:64
  104.1 3.0 %collective-permute-done.20 = f32[216,128]{1,0:T(8,128)S(1)} collective-permute-done((f32[216,128]{1,0:T(8,128)S(1)}, f32[216,128]{1,0:T(8,128)S(1)}, u32[]{:S(2)}, u32[]{:S(2)}) %collective-permute-start.20) | collective-permute-done | bytes 110624 | tf_op jit(solution)/shard_map/ppermute | solution.py:64
  108.6 2.7 %collective-permute-start.23 = (f32[54,128]{1,0:T(8,128)S(1)}, f32[54,128]{1,0:T(8,128)S(1)}, u32[]{:S(2)}, u32[]{:S(2)}) collective-permute-start(f32[54,128]{1,0:T(8,128)S(1)} %get-tuple-element.181), channel_id=1, source_target_pairs={{0,128},{64,192},{128,0},{192,64},{1,129},{65,193},{129,1},{193,65... | collective-permute-start | bytes 82952 | tf_op jit(solution)/shard_map/ppermute | solution.py:64
  115.2 6.0 %collective-permute-start.25 = (f32[54,128]{1,0:T(8,128)S(1)}, f32[54,128]{1,0:T(8,128)S(1)}, u32[]{:S(2)}, u32[]{:S(2)}) collective-permute-start(f32[54,128]{1,0:T(8,128)S(1)} %fusion.37), channel_id=1, source_target_pairs={{0,8},{8,0},{1,9},{9,1},{2,10},{10,2},{3,11},{11,3},{4,12},{12,4},... | collective-permute-start | bytes 82952 | tf_op jit(solution)/shard_map/ppermute | solution.py:91
  121.2 1.9 %collective-permute-done.25 = f32[54,128]{1,0:T(8,128)S(1)} collective-permute-done((f32[54,128]{1,0:T(8,128)S(1)}, f32[54,128]{1,0:T(8,128)S(1)}, u32[]{:S(2)}, u32[]{:S(2)}) %collective-permute-start.25) | collective-permute-done | bytes 27680 | tf_op jit(solution)/shard_map/ppermute | solution.py:91
  124.4 3.0 %collective-permute-start.27 = (f32[54,128]{1,0:T(8,128)S(1)}, f32[54,128]{1,0:T(8,128)S(1)}, u32[]{:S(2)}, u32[]{:S(2)}) collective-permute-start(f32[54,128]{1,0:T(8,128)S(1)} %add.469), channel_id=1, source_target_pairs={{0,128},{64,192},{128,0},{192,64},{1,129},{65,193},{129,1},{193,65... | collective-permute-start | bytes 82952 | tf_op jit(solution)/shard_map/ppermute | solution.py:64
  132.3 2.3 %collective-permute-start.30 = (f32[216,128]{1,0:T(8,128)S(1)}, f32[216,128]{1,0:T(8,128)S(1)}, u32[]{:S(2)}, u32[]{:S(2)}) collective-permute-start(f32[216,128]{1,0:T(8,128)S(1)} %dynamic_update_slice.73), channel_id=1, source_target_pairs={{0,32},{16,48},{32,0},{48,16},{1,33},{17,49},{33,1},{49,17},{2,34}... | collective-permute-start | bytes 331784 | tf_op jit(solution)/shard_map/ppermute | solution.py:64
  136.5 2.1 %collective-permute-done.30 = f32[216,128]{1,0:T(8,128)S(1)} collective-permute-done((f32[216,128]{1,0:T(8,128)S(1)}, f32[216,128]{1,0:T(8,128)S(1)}, u32[]{:S(2)}, u32[]{:S(2)}) %collective-permute-start.30) | collective-permute-done | bytes 110624 | tf_op jit(solution)/shard_map/ppermute | solution.py:64
  142.8 10.6 %collective-permute-start.33 = (f32[128]{0:T(128)S(1)}, f32[128]{0:T(128)S(1)}, u32[]{:S(2)}, u32[]{:S(2)}) collective-permute-start(f32[128]{0:T(128)S(1)} %get-tuple-element.185), channel_id=1, source_target_pairs={{0,3},{1,0},{2,1},{3,2},{4,7},{5,4},{6,5},{7,6},{8,11},{9,8},{10,9... | collective-permute-start | bytes 1544 | tf_op jit(solution)/shard_map/ppermute | solution.py:64
  154.7 3.2 %collective-permute-done.34 = f32[128]{0:T(128)S(1)} collective-permute-done((f32[128]{0:T(128)S(1)}, f32[128]{0:T(128)S(1)}, u32[]{:S(2)}, u32[]{:S(2)}) %collective-permute-start.34) | collective-permute-done | bytes 544 | tf_op jit(solution)/shard_map/ppermute | solution.py:64
  157.9 2.0 %collective-permute-done.35 = f32[128]{0:T(128)S(1)} collective-permute-done((f32[128]{0:T(128)S(1)}, f32[128]{0:T(128)S(1)}, u32[]{:S(2)}, u32[]{:S(2)}) %collective-permute-start.35) | collective-permute-done | bytes 544 | tf_op jit(solution)/shard_map/ppermute | solution.py:64
  (158 shorter events, 61.4 us)
Async XLA Ops:
  13.0 15.9 %collective-permute-start = (bf16[1736,128]{1,0:T(8,128)(2,1)S(1)}, bf16[1736,128]{1,0:T(8,128)(2,1)S(1)}, u32[]{:S(2)}, u32[]{:S(2)}) collective-permute-start(bf16[1736,128]{1,0:T(8,128)(2,1)S(1)} %concatenate.6), channel_id=1, source_target_pairs={{0,1},{1,2},{2,3},{3,0},{4,5},{5,6},{6,7},{7,4},{8,9},{9,10},{10,1... | collective-permute-start | bytes 1333256 | tf_op jit(solution)/shard_map/ppermute | solution.py:64
  15.0 32.1 %collective-permute-start.1 = (bf16[1736,128]{1,0:T(8,128)(2,1)S(1)}, bf16[1736,128]{1,0:T(8,128)(2,1)S(1)}, u32[]{:S(2)}, u32[]{:S(2)}) collective-permute-start(bf16[1736,128]{1,0:T(8,128)(2,1)S(1)} %concatenate.6), channel_id=1, source_target_pairs={{0,2},{1,3},{2,0},{3,1},{4,6},{5,7},{6,4},{7,5},{8,10},{9,11},{10,... | collective-permute-start | bytes 1333256 | tf_op jit(solution)/shard_map/ppermute | solution.py:64
  18.3 28.8 %collective-permute-start.2 = (bf16[1736,128]{1,0:T(8,128)(2,1)S(1)}, bf16[1736,128]{1,0:T(8,128)(2,1)S(1)}, u32[]{:S(2)}, u32[]{:S(2)}) collective-permute-start(bf16[1736,128]{1,0:T(8,128)(2,1)S(1)} %concatenate.6), channel_id=1, source_target_pairs={{0,3},{1,0},{2,1},{3,2},{4,7},{5,4},{6,5},{7,6},{8,11},{9,8},{10,9... | collective-permute-start | bytes 1333256 | tf_op jit(solution)/shard_map/ppermute | solution.py:64
  50.6 5.2 %collective-permute-start.4 = (f32[216,128]{1,0:T(8,128)S(1)}, f32[216,128]{1,0:T(8,128)S(1)}, u32[]{:S(2)}, u32[]{:S(2)}) collective-permute-start(f32[216,128]{1,0:T(8,128)S(1)} %get-tuple-element.176), channel_id=1, source_target_pairs={{0,16},{16,32},{32,48},{48,0},{1,17},{17,33},{33,49},{49,1},{2,18}... | collective-permute-start | bytes 331784 | tf_op jit(solution)/shard_map/ppermute | solution.py:64
  52.2 7.4 %collective-permute-start.5 = (f32[216,128]{1,0:T(8,128)S(1)}, f32[216,128]{1,0:T(8,128)S(1)}, u32[]{:S(2)}, u32[]{:S(2)}) collective-permute-start(f32[216,128]{1,0:T(8,128)S(1)} %get-tuple-element.178), channel_id=1, source_target_pairs={{0,32},{16,48},{32,0},{48,16},{1,33},{17,49},{33,1},{49,17},{2,34}... | collective-permute-start | bytes 331784 | tf_op jit(solution)/shard_map/ppermute | solution.py:64
  53.3 6.9 %collective-permute-start.6 = (f32[216,128]{1,0:T(8,128)S(1)}, f32[216,128]{1,0:T(8,128)S(1)}, u32[]{:S(2)}, u32[]{:S(2)}) collective-permute-start(f32[216,128]{1,0:T(8,128)S(1)} %get-tuple-element.177), channel_id=1, source_target_pairs={{0,48},{16,0},{32,16},{48,32},{1,49},{17,1},{33,17},{49,33},{2,50}... | collective-permute-start | bytes 331784 | tf_op jit(solution)/shard_map/ppermute | solution.py:64
  60.3 5.9 %collective-permute-start.7 = (f32[54,128]{1,0:T(8,128)S(1)}, f32[54,128]{1,0:T(8,128)S(1)}, u32[]{:S(2)}, u32[]{:S(2)}) collective-permute-start(f32[54,128]{1,0:T(8,128)S(1)} %get-tuple-element.182), channel_id=1, source_target_pairs={{0,64},{64,128},{128,192},{192,0},{1,65},{65,129},{129,193},{193,1... | collective-permute-start | bytes 82952 | tf_op jit(solution)/shard_map/ppermute | solution.py:64
  61.9 5.4 %collective-permute-start.8 = (f32[54,128]{1,0:T(8,128)S(1)}, f32[54,128]{1,0:T(8,128)S(1)}, u32[]{:S(2)}, u32[]{:S(2)}) collective-permute-start(f32[54,128]{1,0:T(8,128)S(1)} %get-tuple-element.184), channel_id=1, source_target_pairs={{0,128},{64,192},{128,0},{192,64},{1,129},{65,193},{129,1},{193,65... | collective-permute-start | bytes 82952 | tf_op jit(solution)/shard_map/ppermute | solution.py:64
  68.7 8.0 %collective-permute-start.10 = (f32[54,128]{1,0:T(8,128)S(1)}, f32[54,128]{1,0:T(8,128)S(1)}, u32[]{:S(2)}, u32[]{:S(2)}) collective-permute-start(f32[54,128]{1,0:T(8,128)S(1)} %fusion.39), channel_id=1, source_target_pairs={{0,8},{8,0},{1,9},{9,1},{2,10},{10,2},{3,11},{11,3},{4,12},{12,4},... | collective-permute-start | bytes 82952 | tf_op jit(solution)/shard_map/ppermute | solution.py:91
  76.8 5.1 %collective-permute-start.11 = (f32[54,128]{1,0:T(8,128)S(1)}, f32[54,128]{1,0:T(8,128)S(1)}, u32[]{:S(2)}, u32[]{:S(2)}) collective-permute-start(f32[54,128]{1,0:T(8,128)S(1)} %add.444), channel_id=1, source_target_pairs={{0,64},{64,128},{128,192},{192,0},{1,65},{65,129},{129,193},{193,1... | collective-permute-start | bytes 82952 | tf_op jit(solution)/shard_map/ppermute | solution.py:64
  76.9 6.0 %collective-permute-start.12 = (f32[54,128]{1,0:T(8,128)S(1)}, f32[54,128]{1,0:T(8,128)S(1)}, u32[]{:S(2)}, u32[]{:S(2)}) collective-permute-start(f32[54,128]{1,0:T(8,128)S(1)} %add.444), channel_id=1, source_target_pairs={{0,128},{64,192},{128,0},{192,64},{1,129},{65,193},{129,1},{193,65... | collective-permute-start | bytes 82952 | tf_op jit(solution)/shard_map/ppermute | solution.py:64
  86.4 6.4 %collective-permute-start.15 = (f32[216,128]{1,0:T(8,128)S(1)}, f32[216,128]{1,0:T(8,128)S(1)}, u32[]{:S(2)}, u32[]{:S(2)}) collective-permute-start(f32[216,128]{1,0:T(8,128)S(1)} %dynamic_update_slice.63), channel_id=1, source_target_pairs={{0,32},{16,48},{32,0},{48,16},{1,33},{17,49},{33,1},{49,17},{2,34}... | collective-permute-start | bytes 331784 | tf_op jit(solution)/shard_map/ppermute | solution.py:64
  87.8 5.9 %collective-permute-start.16 = (f32[216,128]{1,0:T(8,128)S(1)}, f32[216,128]{1,0:T(8,128)S(1)}, u32[]{:S(2)}, u32[]{:S(2)}) collective-permute-start(f32[216,128]{1,0:T(8,128)S(1)} %dynamic_update_slice.63), channel_id=1, source_target_pairs={{0,48},{16,0},{32,16},{48,32},{1,49},{17,1},{33,17},{49,33},{2,50}... | collective-permute-start | bytes 331784 | tf_op jit(solution)/shard_map/ppermute | solution.py:64
  99.0 5.2 %collective-permute-start.19 = (f32[216,128]{1,0:T(8,128)S(1)}, f32[216,128]{1,0:T(8,128)S(1)}, u32[]{:S(2)}, u32[]{:S(2)}) collective-permute-start(f32[216,128]{1,0:T(8,128)S(1)} %get-tuple-element.173), channel_id=1, source_target_pairs={{0,16},{16,32},{32,48},{48,0},{1,17},{17,33},{33,49},{49,1},{2,18}... | collective-permute-start | bytes 331784 | tf_op jit(solution)/shard_map/ppermute | solution.py:64
  99.7 7.4 %collective-permute-start.20 = (f32[216,128]{1,0:T(8,128)S(1)}, f32[216,128]{1,0:T(8,128)S(1)}, u32[]{:S(2)}, u32[]{:S(2)}) collective-permute-start(f32[216,128]{1,0:T(8,128)S(1)} %get-tuple-element.175), channel_id=1, source_target_pairs={{0,32},{16,48},{32,0},{48,16},{1,33},{17,49},{33,1},{49,17},{2,34}... | collective-permute-start | bytes 331784 | tf_op jit(solution)/shard_map/ppermute | solution.py:64
  101.6 6.8 %collective-permute-start.21 = (f32[216,128]{1,0:T(8,128)S(1)}, f32[216,128]{1,0:T(8,128)S(1)}, u32[]{:S(2)}, u32[]{:S(2)}) collective-permute-start(f32[216,128]{1,0:T(8,128)S(1)} %get-tuple-element.174), channel_id=1, source_target_pairs={{0,48},{16,0},{32,16},{48,32},{1,49},{17,1},{33,17},{49,33},{2,50}... | collective-permute-start | bytes 331784 | tf_op jit(solution)/shard_map/ppermute | solution.py:64
  108.5 5.2 %collective-permute-start.22 = (f32[54,128]{1,0:T(8,128)S(1)}, f32[54,128]{1,0:T(8,128)S(1)}, u32[]{:S(2)}, u32[]{:S(2)}) collective-permute-start(f32[54,128]{1,0:T(8,128)S(1)} %get-tuple-element.179), channel_id=1, source_target_pairs={{0,64},{64,128},{128,192},{192,0},{1,65},{65,129},{129,193},{193,1... | collective-permute-start | bytes 82952 | tf_op jit(solution)/shard_map/ppermute | solution.py:64
  108.6 5.4 %collective-permute-start.23 = (f32[54,128]{1,0:T(8,128)S(1)}, f32[54,128]{1,0:T(8,128)S(1)}, u32[]{:S(2)}, u32[]{:S(2)}) collective-permute-start(f32[54,128]{1,0:T(8,128)S(1)} %get-tuple-element.181), channel_id=1, source_target_pairs={{0,128},{64,192},{128,0},{192,64},{1,129},{65,193},{129,1},{193,65... | collective-permute-start | bytes 82952 | tf_op jit(solution)/shard_map/ppermute | solution.py:64
  115.2 7.9 %collective-permute-start.25 = (f32[54,128]{1,0:T(8,128)S(1)}, f32[54,128]{1,0:T(8,128)S(1)}, u32[]{:S(2)}, u32[]{:S(2)}) collective-permute-start(f32[54,128]{1,0:T(8,128)S(1)} %fusion.37), channel_id=1, source_target_pairs={{0,8},{8,0},{1,9},{9,1},{2,10},{10,2},{3,11},{11,3},{4,12},{12,4},... | collective-permute-start | bytes 82952 | tf_op jit(solution)/shard_map/ppermute | solution.py:91
  124.4 5.4 %collective-permute-start.27 = (f32[54,128]{1,0:T(8,128)S(1)}, f32[54,128]{1,0:T(8,128)S(1)}, u32[]{:S(2)}, u32[]{:S(2)}) collective-permute-start(f32[54,128]{1,0:T(8,128)S(1)} %add.469), channel_id=1, source_target_pairs={{0,128},{64,192},{128,0},{192,64},{1,129},{65,193},{129,1},{193,65... | collective-permute-start | bytes 82952 | tf_op jit(solution)/shard_map/ppermute | solution.py:64
  132.3 6.3 %collective-permute-start.30 = (f32[216,128]{1,0:T(8,128)S(1)}, f32[216,128]{1,0:T(8,128)S(1)}, u32[]{:S(2)}, u32[]{:S(2)}) collective-permute-start(f32[216,128]{1,0:T(8,128)S(1)} %dynamic_update_slice.73), channel_id=1, source_target_pairs={{0,32},{16,48},{32,0},{48,16},{1,33},{17,49},{33,1},{49,17},{2,34}... | collective-permute-start | bytes 331784 | tf_op jit(solution)/shard_map/ppermute | solution.py:64
  134.6 5.1 %collective-permute-start.31 = (f32[216,128]{1,0:T(8,128)S(1)}, f32[216,128]{1,0:T(8,128)S(1)}, u32[]{:S(2)}, u32[]{:S(2)}) collective-permute-start(f32[216,128]{1,0:T(8,128)S(1)} %dynamic_update_slice.73), channel_id=1, source_target_pairs={{0,48},{16,0},{32,16},{48,32},{1,49},{17,1},{33,17},{49,33},{2,50}... | collective-permute-start | bytes 331784 | tf_op jit(solution)/shard_map/ppermute | solution.py:64
  142.8 11.9 %collective-permute-start.33 = (f32[128]{0:T(128)S(1)}, f32[128]{0:T(128)S(1)}, u32[]{:S(2)}, u32[]{:S(2)}) collective-permute-start(f32[128]{0:T(128)S(1)} %get-tuple-element.185), channel_id=1, source_target_pairs={{0,3},{1,0},{2,1},{3,2},{4,7},{5,4},{6,5},{7,6},{8,11},{9,8},{10,9... | collective-permute-start | bytes 1544 | tf_op jit(solution)/shard_map/ppermute | solution.py:64
  154.5 5.4 %collective-permute-start.35 = (f32[128]{0:T(128)S(1)}, f32[128]{0:T(128)S(1)}, u32[]{:S(2)}, u32[]{:S(2)}) collective-permute-start(f32[128]{0:T(128)S(1)} %get-tuple-element.186), channel_id=1, source_target_pairs={{0,1},{1,2},{2,3},{3,0},{4,5},{5,6},{6,7},{7,4},{8,9},{9,10},{10,1... | collective-permute-start | bytes 1544 | tf_op jit(solution)/shard_map/ppermute | solution.py:64
  (19 other events, 74.4 us)
